TPU v7x, 256 devices: a whole 4x4x8 slice. The times are simulated.
256 devices in a mesh: row: 16 (over z, core), col: 16 (over x, y).
Axes of the slice: x: 4, y: 4, z: 8, core: 2. Of those that a mesh axis runs over, the one named last changes fastest.
Arguments:
- site_tensor: bfloat16 [1024, 4, 1024], P('row', None, 'col'), may hold values from -180 to 180
- site_tangent: bfloat16 [1024, 4, 1024], P('row', None, 'col'), may hold values from -180 to 180
- left_env: bfloat16 [1024, 16384], P('row', 'col'), may hold values from -0.1875 to 0.375
- right_env: bfloat16 [1024, 16384], P('row', 'col'), may hold values from -0.046875 to 0.09375
- mpo: bfloat16 [16, 16, 4, 4], replicated, may hold values from -0.25 to 0.75
- dissipation: float32 [4], replicated, may hold values from 0.2 to 2
Outputs:
- evolved: float32 [1024, 4, 1024], P('row', None, 'col')
- evolved_tangent: float32 [1024, 4, 1024], P('row', None, 'col')
All inputs are finite; a program needn't handle non-finite values.
Results may differ from a plain program's by a relative error of at most 0.0055.
Values may be sent and summed in bfloat16 or wider, within the bound.
No kernel may reach another device: no remote copies, remote signals or barrier semaphores. Data moves between devices by JAX's collectives and lax.ppermute only.
A program may use at most 64 MiB of HBM per device.

v0:
```python
import jax
import jax.numpy as jnp
from jax import lax
from jax.sharding import PartitionSpec as P

KRYLOV = 3
taylor_order = 16


def inner(first, second):
    return jnp.sum(first * second)


def total(values):
    return lax.psum(lax.psum(values, "col"), "row")


def taylor(hess, dhess):
    size = hess.shape[0]
    term = jnp.zeros((size,), jnp.float32).at[0].set(1.0)
    dterm = jnp.zeros((size,), jnp.float32)
    total = term
    dtotal = dterm
    for order in range(1, taylor_order + 1):
        nterm = jnp.dot(hess, term, precision=lax.Precision.HIGHEST) / order
        dterm = (
            jnp.dot(dhess, term, precision=lax.Precision.HIGHEST)
            + jnp.dot(hess, dterm, precision=lax.Precision.HIGHEST)
        ) / order
        term = nterm
        total = total + term
        dtotal = dtotal + dterm
    return (total, dtotal)


def local(site_tensor, site_tangent, left_env, right_env, mpo, dissipation):
    rows_here, physical, cols_here = site_tensor.shape
    channels = mpo.shape[0]
    left_whole = lax.all_gather(left_env, "col", axis=1, tiled=True)
    right_whole = lax.all_gather(right_env, "row", axis=0, tiled=True)

    def apply(stacked):
        panels = stacked.shape[1]
        whole = lax.all_gather(stacked.astype(jnp.bfloat16), "row", axis=0, tiled=True)
        flat = whole.reshape(whole.shape[0], panels * physical * cols_here)
        left_three = left_whole.reshape(rows_here, flat.shape[0], channels)
        mixed = lax.dot_general(
            left_three, flat, (((1,), (0,)), ((), ())), preferred_element_type=jnp.float32
        )
        mixed = mixed.astype(jnp.bfloat16).reshape(rows_here, channels, panels, physical, cols_here)
        channel = jnp.einsum("awspr,wvpq->asqrv", mixed, mpo, preferred_element_type=jnp.float32)
        channel = channel.astype(jnp.bfloat16).reshape(
            rows_here * panels * physical, cols_here * channels
        )
        partial_rows = lax.dot_general(
            channel, right_whole, (((1,), (1,)), ((), ())), preferred_element_type=jnp.float32
        )
        partial_rows = partial_rows.reshape(rows_here, panels, physical, partial_rows.shape[1])
        summed = lax.psum_scatter(partial_rows, "col", scatter_dimension=3, tiled=True)
        return summed - dissipation[None, None, :, None] * stacked

    primal = site_tensor.astype(jnp.float32)
    tangent = site_tangent.astype(jnp.float32)
    starting = total(jnp.stack([inner(primal, primal), inner(primal, tangent)]))
    norm_site = jnp.sqrt(starting[0])
    norm_tangent = starting[1] / norm_site
    basis = [primal / norm_site]
    tangents = [(tangent - basis[0] * norm_tangent) / norm_site]
    hess = jnp.zeros((KRYLOV, KRYLOV), jnp.float32)
    dhess = jnp.zeros((KRYLOV, KRYLOV), jnp.float32)
    gram = jnp.zeros((KRYLOV, KRYLOV), jnp.float32)
    cross = jnp.zeros((KRYLOV, KRYLOV), jnp.float32)
    for level in range(KRYLOV):
        both = apply(jnp.stack([basis[level], tangents[level]], axis=1))
        image = both[:, 0]
        dimage = both[:, 1]
        counted = level + 1
        locals_list = [inner(vector, image) for vector in basis]
        locals_list = locals_list + [inner(vector, image) for vector in tangents]
        locals_list = locals_list + [inner(vector, dimage) for vector in basis]
        last = level + 1 == KRYLOV
        if not last:
            newest = basis[level]
            locals_list = locals_list + [inner(image, image), inner(image, dimage)]
            locals_list = locals_list + [inner(newest, vector) for vector in basis]
            locals_list = locals_list + [inner(newest, vector) for vector in tangents]
            locals_list = locals_list + [inner(vector, tangents[level]) for vector in basis[:level]]
        totals = total(jnp.stack(locals_list))
        coeffs = totals[:counted]
        across = totals[counted : 2 * counted]
        along = totals[2 * counted : 3 * counted]
        dcoeffs = across + along
        hess = hess.at[:counted, level].set(coeffs)
        dhess = dhess.at[:counted, level].set(dcoeffs)
        if not last:
            at = 3 * counted
            squared_image = totals[at]
            image_dimage = totals[at + 1]
            at += 2
            gram = gram.at[level, :counted].set(totals[at : at + counted])
            gram = gram.at[:counted, level].set(totals[at : at + counted])
            at += counted
            cross = cross.at[level, :counted].set(totals[at : at + counted])
            at += counted
            cross = cross.at[:level, level].set(totals[at : at + level])
            g = gram[:counted, :counted]
            t = cross[:counted, :counted]
            squared = (
                squared_image
                - 2.0 * jnp.sum(coeffs * coeffs)
                + jnp.dot(
                    coeffs,
                    jnp.dot(g, coeffs, precision=lax.Precision.HIGHEST),
                    precision=lax.Precision.HIGHEST,
                )
            )
            mixed_term = (
                image_dimage
                - jnp.sum(dcoeffs * coeffs)
                - jnp.sum(coeffs * across)
                - jnp.sum(coeffs * along)
                + jnp.dot(
                    coeffs,
                    jnp.dot(g, dcoeffs, precision=lax.Precision.HIGHEST),
                    precision=lax.Precision.HIGHEST,
                )
                + jnp.dot(
                    coeffs,
                    jnp.dot(t, coeffs, precision=lax.Precision.HIGHEST),
                    precision=lax.Precision.HIGHEST,
                )
            )
            residual = image
            dresidual = dimage
            for index in range(counted):
                residual = residual - coeffs[index] * basis[index]
                dresidual = (
                    dresidual - dcoeffs[index] * basis[index] - coeffs[index] * tangents[index]
                )
            height = jnp.sqrt(squared)
            dheight = mixed_term / height
            newvec = residual / height
            basis.append(newvec)
            tangents.append((dresidual - newvec * dheight) / height)
            hess = hess.at[level + 1, level].set(height)
            dhess = dhess.at[level + 1, level].set(dheight)
    coeff, dcoeff = taylor(hess, dhess)
    spread = jnp.zeros_like(primal)
    dspread = jnp.zeros_like(primal)
    for index in range(KRYLOV):
        spread = spread + coeff[index] * basis[index]
        dspread = dspread + coeff[index] * tangents[index] + dcoeff[index] * basis[index]
    evolved = norm_site * spread
    evolved_tangent = norm_tangent * spread + norm_site * dspread
    return (evolved, evolved_tangent)


def solution(mesh):
    in_specs = (
        P("row", None, "col"),
        P("row", None, "col"),
        P("row", "col"),
        P("row", "col"),
        P(),
        P(),
    )
    out_specs = (P("row", None, "col"), P("row", None, "col"))
    return jax.shard_map(local, mesh=mesh, in_specs=in_specs, out_specs=out_specs, check_vma=False)
```

profile of v0, /device:TPU:1, one launch (start us, length us, event | category | flops | bytes accessed | tf_op | source)
XLA Modules:
  0.0 870.2 jit_solution(10881828648179970118)
XLA Ops:
  7.2 1.5 fusion.79
  8.7 1.4 pad_maximum_fusion.3
  10.1 34.2 %psum.56 = f32[2]{0:T(128)S(1)} all-reduce(f32[2]{0:T(128)S(1)} %pad_maximum_fusion.3), channel_id=1, replica_groups=mesh['row'=16,'col'=16] {'col'}, use_global_device_ids=true, to_apply=%region_2.0 | all-reduce | flops 2 | bytes 16 | tf_op jit(solution)/shard_map/psum | solution.py:15
  44.3 33.8 %psum.57 = f32[2]{0:T(128)S(1)} all-reduce(f32[2]{0:T(128)S(1)} %psum.56), channel_id=1, replica_groups=mesh['row'=16,'col'=16] {'row'}, use_global_device_ids=true, to_apply=%region_3.0 | all-reduce | flops 2 | bytes 16 | tf_op jit(solution)/shard_map/psum | solution.py:15
  80.1 0.9 fusion.138
  83.3 1.0 copy.138
  84.3 32.3 %all-gather.6.cloned.1.call-done = bf16[1024,2,4,64]{3,2,1,0:T(4,128)(2,1)} async-done(((bf16[64,2,4,64]{3,2,1,0:T(4,128)(2,1)}), bf16[1024,2,4,64]{3,2,1,0:T(4,128)(2,1)}) %all-gather.6.cloned.1.call-update) | async-done | bytes 1048592 | tf_op jit(solution)/shard_map/all_gather | solution.py:44
  116.6 4.1 copy.109
  120.7 44.7 %all-gather.8.cloned.1.call-done = bf16[64,16384]{1,0:T(8,128)(2,1)} async-done(((bf16[64,1024]{1,0:T(8,128)(2,1)}), bf16[64,16384]{1,0:T(8,128)(2,1)}) %all-gather.8.cloned.1.call-update) | async-done | bytes 2097168 | tf_op jit(solution)/shard_map/all_gather | solution.py:39
  165.5 4.8 copy.110
  170.2 4.5 copy.112
  174.7 3.5 fusion.18
  178.2 4.7 reshape.536
  182.9 4.7 fusion.9
  187.6 5.8 copy.115
  193.4 14.8 %all-gather.10.cloned.1.call-done = bf16[1024,1024]{1,0:T(8,128)(2,1)} async-done(((bf16[64,1024]{1,0:T(8,128)(2,1)}), bf16[1024,1024]{1,0:T(8,128)(2,1)}) %all-gather.10.cloned.1.call-update) | async-done | bytes 2097168 | tf_op jit(solution)/shard_map/all_gather | solution.py:40
  208.1 6.0 fusion.5
  214.1 4.8 copy.173
  218.9 5.6 reshape.685
  225.0 76.2 %reduce-scatter.10.cloned.1.call-done = f32[64,512]{1,0:T(8,128)} async-done(((f32[1024,512]{1,0:T(8,128)}), f32[64,512]{1,0:T(8,128)}) %reduce-scatter.10.cloned.1.call-update) | async-done | bytes 131088
  301.2 1.1 reshape.686
  302.6 0.8 multiply_reduce_fusion.24
  303.4 4.5 stack.145
  307.8 30.9 %psum.58 = f32[7]{0:T(128)S(1)} all-reduce(f32[7]{0:T(128)S(1)} %stack.145), channel_id=1, replica_groups=mesh['row'=16,'col'=16] {'col'}, use_global_device_ids=true, to_apply=%region_12.0 | all-reduce | flops 7 | bytes 56 | tf_op jit(solution)/shard_map/psum | solution.py:15
  338.7 32.9 %psum.59 = f32[7]{0:T(128)S(1)} all-reduce(f32[7]{0:T(128)S(1)} %psum.58), channel_id=1, replica_groups=mesh['row'=16,'col'=16] {'row'}, use_global_device_ids=true, to_apply=%region_13.0 | all-reduce | flops 7 | bytes 56 | tf_op jit(solution)/shard_map/psum | solution.py:15
  384.9 35.9 %all-gather.12.cloned.1.call-done = bf16[1024,2,4,64]{3,2,1,0:T(4,128)(2,1)} async-done(((bf16[64,2,4,64]{3,2,1,0:T(4,128)(2,1)}), bf16[1024,2,4,64]{3,2,1,0:T(4,128)(2,1)}) %all-gather.12.cloned.1.call-update) | async-done | bytes 1048592 | tf_op jit(solution)/shard_map/all_gather | solution.py:44
  420.8 4.1 copy.118
  424.9 3.5 fusion.19
  428.4 4.7 reshape.543
  433.1 4.7 fusion.12
  437.7 5.8 copy.123
  443.5 6.0 fusion.3
  449.5 4.8 copy.175
  454.3 5.6 reshape.687
  462.4 74.2 %reduce-scatter.12.cloned.1.call-done = f32[64,512]{1,0:T(8,128)} async-done(((f32[1024,512]{1,0:T(8,128)}), f32[64,512]{1,0:T(8,128)}) %reduce-scatter.12.cloned.1.call-update) | async-done | bytes 131088
  536.6 1.1 reshape.688
  538.0 0.9 multiply_reduce_fusion.14
  538.8 8.2 stack.162
  547.7 30.9 %psum.60 = f32[13]{0:T(128)S(1)} all-reduce(f32[13]{0:T(128)S(1)} %stack.162), channel_id=1, replica_groups=mesh['row'=16,'col'=16] {'col'}, use_global_device_ids=true, to_apply=%region_28.0 | all-reduce | flops 13 | bytes 104 | tf_op jit(solution)/shard_map/psum | solution.py:15
  578.6 33.1 %psum.61 = f32[13]{0:T(128)S(1)} all-reduce(f32[13]{0:T(128)S(1)} %psum.60), channel_id=1, replica_groups=mesh['row'=16,'col'=16] {'row'}, use_global_device_ids=true, to_apply=%region_29.0 | all-reduce | flops 13 | bytes 104 | tf_op jit(solution)/shard_map/psum | solution.py:15
  612.3 0.8 slice_bitcast_fusion.10
  613.3 1.5 scatter.70
  614.8 0.8 fusion.74
  617.0 1.8 dynamic-slice.126
  620.5 1.3 scatter.76
  628.2 2.7 subtract_divide_fusion
  631.7 35.9 %all-gather.14.cloned.1.call-done = bf16[1024,2,4,64]{3,2,1,0:T(4,128)(2,1)} async-done(((bf16[64,2,4,64]{3,2,1,0:T(4,128)(2,1)}), bf16[1024,2,4,64]{3,2,1,0:T(4,128)(2,1)}) %all-gather.14.cloned.1.call-update) | async-done | bytes 1048592 | tf_op jit(solution)/shard_map/all_gather | solution.py:44
  667.6 4.1 copy.127
  671.7 3.5 fusion.20
  675.2 3.5 reshape.554
  678.8 3.1 fusion.15
  681.8 5.8 copy.132
  687.6 4.6 fusion.1
  692.3 3.2 copy.177
  695.5 5.6 reshape.689
  702.2 1.4 scatter.64
  703.5 1.4 scatter.85
  704.9 73.0 %reduce-scatter.14.cloned.1.call-done = f32[64,512]{1,0:T(8,128)} async-done(((f32[1024,512]{1,0:T(8,128)}), f32[64,512]{1,0:T(8,128)}) %reduce-scatter.14.cloned.1.call-update) | async-done | bytes 131088
  777.9 1.1 reshape.690
  779.2 0.9 multiply_reduce_fusion
  780.0 5.7 stack.175
  785.9 30.9 %psum.62 = f32[9]{0:T(128)S(1)} all-reduce(f32[9]{0:T(128)S(1)} %stack.175), channel_id=1, replica_groups=mesh['row'=16,'col'=16] {'col'}, use_global_device_ids=true, to_apply=%region_45.0 | all-reduce | flops 9 | bytes 72 | tf_op jit(solution)/shard_map/psum | solution.py:15
  816.9 32.9 %psum.63 = f32[9]{0:T(128)S(1)} all-reduce(f32[9]{0:T(128)S(1)} %psum.62), channel_id=1, replica_groups=mesh['row'=16,'col'=16] {'row'}, use_global_device_ids=true, to_apply=%region_46.0 | all-reduce | flops 9 | bytes 72 | tf_op jit(solution)/shard_map/psum | solution.py:15
  857.8 3.9 multiply_add_fusion
  (114 shorter events, 24.1 us)
Async XLA Ops:
  7.2 109.4 %all-gather.6.cloned.1.call-start = ((), (), s32[]{:S(2)}) async-start(), calls=%async_computation.3 | async-start | bytes 2228224 | tf_op jit(solution)/shard_map/all_gather | solution.py:44
  81.8 83.7 %all-gather.8.cloned.1.call-start = ((), (), s32[]{:S(2)}) async-start(), calls=%async_computation.4 | async-start | bytes 2228224 | tf_op jit(solution)/shard_map/all_gather | solution.py:39
  82.5 125.6 %all-gather.10.cloned.1.call-start = ((), (), s32[]{:S(2)}) async-start(), calls=%async_computation.5 | async-start | bytes 2228224 | tf_op jit(solution)/shard_map/all_gather | solution.py:40
  83.3 218.0 %reduce-scatter.10.cloned.1.call-start = ((), (), s32[]{:S(2)}) async-start(), calls=%async_computation.8 | async-start | bytes 2228224
  224.5 78.0 %copy-start.2 = (f32[4]{0:T(128)S(1)}, f32[4]{0:T(128)}, u32[]{:S(2)}) copy-start(f32[4]{0:T(128)} %param.47) | copy-start | bytes 52
  224.5 78.1 %copy-start = (bf16[64,4,64]{2,1,0:T(4,128)(2,1)S(1)}, bf16[64,4,64]{2,1,0:T(4,128)(2,1)}, u32[]{:S(2)}) copy-start(bf16[64,4,64]{2,1,0:T(4,128)(2,1)} %param.42) | copy-start | bytes 98308
  224.5 78.1 %copy-start.1 = (bf16[64,4,64]{2,1,0:T(4,128)(2,1)S(1)}, bf16[64,4,64]{2,1,0:T(4,128)(2,1)}, u32[]{:S(2)}) copy-start(bf16[64,4,64]{2,1,0:T(4,128)(2,1)} %param.43) | copy-start | bytes 98308
  224.5 196.3 %all-gather.12.cloned.1.call-start = ((), (), s32[]{:S(2)}) async-start(), calls=%async_computation.6 | async-start | bytes 2228224 | tf_op jit(solution)/shard_map/all_gather | solution.py:44
  384.8 151.8 %reduce-scatter.12.cloned.1.call-start = ((), (), s32[]{:S(2)}) async-start(), calls=%async_computation.9 | async-start | bytes 2228224
  459.9 207.7 %all-gather.14.cloned.1.call-start = ((), (), s32[]{:S(2)}) async-start(), calls=%async_computation.7 | async-start | bytes 2228224 | tf_op jit(solution)/shard_map/all_gather | solution.py:44
  631.7 146.2 %reduce-scatter.14.cloned.1.call-start = ((), (), s32[]{:S(2)}) async-start(), calls=%async_computation.10 | async-start | bytes 2228224
  701.1 148.9 %copy-start.3 = (f32[3,1]{0,1:T(1,128)S(1)}, f32[3,1]{0,1:T(1,128)}, u32[]{:S(2)}) copy-start(f32[3,1]{0,1:T(1,128)} %constant.468) | copy-start | bytes 40
Sparse Core Ops, SparseCore 0:
  81.9 34.6 all-gather.5
  119.1 46.3 all-gather.7
  167.3 40.7 all-gather.9
  224.6 76.5 reduce-scatter.9
  385.0 35.7 all-gather.11
  460.0 76.5 reduce-scatter.11
  631.8 35.7 all-gather.13
  701.2 76.6 reduce-scatter.13
where the time goes:
time: 881 us; the launch traced here: 870 us
  waiting for transfers between devices  388 us (44%)
  blocking collectives  260 us (30%)
  local copies, waits for them, and re-layouts  123 us (14%)
  matrix products  48.2 us (5%)
  between operations  34.5 us (4%)
  other arithmetic  15.4 us (2%)
    psum x8, blocking collectives, total(): return lax.psum(lax.psum(values, 'col'), 'row')  260 us
    unnamed x11, waiting for transfers between devices  225 us
    all_gather x3, waiting for transfers between devices, apply(): lax.all_gather(stacked.astype(jnp.bfloat16), 'row', axis=0, tiled=True)  104 us
    all_gather x1, waiting for transfers between devices, local(): left_whole = lax.all_gather(left_env, 'col', axis=1, tiled=True)  44.7 us
    unnamed x23, local copies, waits for them, and re-layouts  35.7 us
    another operation x3, local copies, waits for them, and re-layouts, local(): totals = total(jnp.stack(locals_list))  18.4 us
  transfers between devices with their start and end apart: 8, of which 8 were waited for; matrix products, arithmetic and copies ran while one was open for 5% of the time, Pallas kernels for 0%

commit v1 on v0

--- a/solution.py
+++ b/solution.py
@@ -41,7 +41,12 @@
 
     def apply(stacked):
         panels = stacked.shape[1]
-        whole = lax.all_gather(stacked.astype(jnp.bfloat16), "row", axis=0, tiled=True)
+        whole = jnp.concatenate(
+            lax.all_to_all(
+                jnp.stack([stacked.astype(jnp.bfloat16)] * lax.axis_size("row")), "row", 0, 0
+            ),
+            axis=0,
+        )
         flat = whole.reshape(whole.shape[0], panels * physical * cols_here)
         left_three = left_whole.reshape(rows_here, flat.shape[0], channels)
         mixed = lax.dot_general(

time: 881 us -> 797 us (0.905)
  waiting for transfers between devices: 388 us -> 238 us
  blocking collectives: 260 us -> 331 us
    all_gather x3 -> x0, waiting for transfers between devices: 104 us -> none  [apply(): lax.all_gather(stacked.astype(jnp.bfloat16), 'row', axis=0, tiled=True)]
    all_to_all x0 -> x2, blocking collectives: none -> 71.5 us  [apply(): lax.all_to_all(jnp.stack([stacked.astype(jnp.bfloat16)] * lax.axis_size('...]
    all_gather x1, waiting for transfers between devices: 44.7 us -> 0.02 us  [local(): left_whole = lax.all_gather(left_env, 'col', axis=1, tiled=True)]
    all_to_all x0 -> x1, waiting for transfers between devices: none -> 28 us  [apply(): lax.all_to_all(jnp.stack([stacked.astype(jnp.bfloat16)] * lax.axis_size('...]
    unnamed x11 -> x8, waiting for transfers between devices: 225 us -> 210 us
    all_gather x1, waiting for transfers between devices: 14.8 us -> 0.01 us  [local(): right_whole = lax.all_gather(right_env, 'row', axis=0, tiled=True)]
    all_gather x3 -> x0, local copies, waits for them, and re-layouts: 12.3 us -> none  [apply(): lax.all_gather(stacked.astype(jnp.bfloat16), 'row', axis=0, tiled=True)]
    unnamed x23 -> x47, local copies, waits for them, and re-layouts: 35.7 us -> 47.8 us
  transfers between devices with their start and end apart: 8 -> 6, of which waited for: 8 -> 4; matrix products, arithmetic and copies ran while one was open for 5% -> 5% of each run, Pallas kernels for 0% -> 0%
where the time goes in v1:
time: 797 us; the launch traced here: 793 us
  blocking collectives  331 us (42%)
  waiting for transfers between devices  238 us (30%)
  local copies, waits for them, and re-layouts  125 us (16%)
  matrix products  42 us (5%)
  between operations  34.6 us (4%)
  other arithmetic  15.3 us (2%)
    psum x8, blocking collectives, total(): return lax.psum(lax.psum(values, 'col'), 'row')  260 us
    unnamed x8, waiting for transfers between devices  210 us
    all_to_all x2, blocking collectives, apply(): lax.all_to_all(jnp.stack([stacked.astype(jnp.bfloat16)] * lax.axis_size('...  71.5 us
    unnamed x47, local copies, waits for them, and re-layouts  47.8 us
    all_to_all x1, waiting for transfers between devices, apply(): lax.all_to_all(jnp.stack([stacked.astype(jnp.bfloat16)] * lax.axis_size('...  28 us
    another operation x3, local copies, waits for them, and re-layouts, local(): totals = total(jnp.stack(locals_list))  18.1 us
  transfers between devices with their start and end apart: 6, of which 4 were waited for; matrix products, arithmetic and copies ran while one was open for 5% of the time, Pallas kernels for 0%

profile of v1, /device:TPU:1, one launch (start us, length us, event | category | flops | bytes accessed | tf_op | source)
XLA Modules:
  0.0 792.7 jit_solution(15295464829394072419)
XLA Ops:
  8.6 1.5 fusion.79
  10.2 1.4 pad_maximum_fusion.3
  11.5 34.3 %psum.56 = f32[2]{0:T(128)S(1)} all-reduce(f32[2]{0:T(128)S(1)} %pad_maximum_fusion.3), channel_id=1, replica_groups=mesh['row'=16,'col'=16] {'col'}, use_global_device_ids=true, to_apply=%region_2.0 | all-reduce | flops 2 | bytes 16 | tf_op jit(solution)/shard_map/psum | solution.py:15
  45.8 34.3 %psum.57 = f32[2]{0:T(128)S(1)} all-reduce(f32[2]{0:T(128)S(1)} %psum.56), channel_id=1, replica_groups=mesh['row'=16,'col'=16] {'row'}, use_global_device_ids=true, to_apply=%region_3.0 | all-reduce | flops 2 | bytes 16 | tf_op jit(solution)/shard_map/psum | solution.py:15
  82.0 0.9 fusion.138
  83.9 2.3 reshape.709
  86.2 6.1 all-to-all-start
  93.0 28.0 %all-to-all-done = bf16[16,2,16384]{2,1,0:T(2,128)(2,1)S(1)} async-done(((bf16[16,2,16384]{2,1,0:T(2,128)(2,1)}), bf16[16,2,16384]{2,1,0:T(2,128)(2,1)S(1)}, u32[]{:S(2)}, u32[]{:S(2)}) %all-to-all-start) | async-done | bytes 1048608 | tf_op jit(solution)/shard_map/all_to_all | solution.py:45
  121.0 1.3 reshape.710
  122.3 1.3 reshape.576
  123.6 4.8 copy.49
  128.4 4.5 copy.50
  132.9 2.2 fusion.18
  135.1 4.7 reshape.553
  139.8 3.4 fusion.9
  143.2 4.2 copy.53
  147.4 4.6 fusion.5
  152.0 3.2 copy.101
  155.2 5.6 reshape.703
  160.9 73.8 %reduce-scatter.10.cloned.1.call-done = f32[64,512]{1,0:T(8,128)} async-done(((f32[1024,512]{1,0:T(8,128)}), f32[64,512]{1,0:T(8,128)}) %reduce-scatter.10.cloned.1.call-update) | async-done | bytes 131088
  234.7 1.1 reshape.704
  236.8 4.3 stack.203
  241.1 30.9 %psum.58 = f32[7]{0:T(128)S(1)} all-reduce(f32[7]{0:T(128)S(1)} %stack.203), channel_id=1, replica_groups=mesh['row'=16,'col'=16] {'col'}, use_global_device_ids=true, to_apply=%region_12.0 | all-reduce | flops 7 | bytes 56 | tf_op jit(solution)/shard_map/psum | solution.py:15
  272.0 32.9 %psum.59 = f32[7]{0:T(128)S(1)} all-reduce(f32[7]{0:T(128)S(1)} %psum.58), channel_id=1, replica_groups=mesh['row'=16,'col'=16] {'row'}, use_global_device_ids=true, to_apply=%region_13.0 | all-reduce | flops 7 | bytes 56 | tf_op jit(solution)/shard_map/psum | solution.py:15
  318.5 1.5 reshape.711
  319.9 35.7 %all_to_all.15 = bf16[16,2,16384]{2,1,0:T(2,128)(2,1)} all-to-all(bf16[16,2,16384]{2,1,0:T(2,128)(2,1)S(1)} %reshape.711), channel_id=1, replica_groups=mesh['row'=16,'col'=16] {'row'}, dimensions={0} | all-to-all | bytes 2097152 | tf_op jit(solution)/shard_map/all_to_all | solution.py:45
  355.6 4.5 reshape.712
  360.1 1.3 reshape.581
  361.3 3.8 fusion.19
  365.2 3.6 reshape.559
  368.8 3.1 fusion.12
  371.9 5.8 copy.59
  377.7 4.6 fusion.3
  382.3 3.2 copy.103
  385.5 5.6 reshape.705
  393.7 67.9 %reduce-scatter.12.cloned.1.call-done = f32[64,512]{1,0:T(8,128)} async-done(((f32[1024,512]{1,0:T(8,128)}), f32[64,512]{1,0:T(8,128)}) %reduce-scatter.12.cloned.1.call-update) | async-done | bytes 131088
  461.6 1.1 reshape.706
  463.8 8.1 %stack.221 = f32[13]{0:T(128)S(1)} concatenate(f32[1]{0:T(128)} %bitcast.44, f32[1]{0:T(128)} %bitcast.45, f32[1]{0:T(128)} %bitcast.46, f32[1]{0:T(128)} %bitcast.47, f32[1]{0:T(128)} %bitcast.49, f32[1]{0:T(128)} %bitcast.50, f32[1]{0:T(128)} %bitcast.51, f32[1]{0:T(128)} %bitcast.52, f32[1]{0:T(128)} %bitcast.53, f32[1]{0:T(128)} %bitcast.54, f32[1]{0:T(128)} %bitcast.55, ...), dimensions={0} | concatenate | bytes 104 | tf_op jit(solution)/shard_map/stack | solution.py:93
  471.9 0.9 scatter.66
  472.8 30.9 %psum.60 = f32[13]{0:T(128)S(1)} all-reduce(f32[13]{0:T(128)S(1)} %stack.221), channel_id=1, replica_groups=mesh['row'=16,'col'=16] {'col'}, use_global_device_ids=true, to_apply=%region_28.0 | all-reduce | flops 13 | bytes 104 | tf_op jit(solution)/shard_map/psum | solution.py:15
  503.7 32.9 %psum.61 = f32[13]{0:T(128)S(1)} all-reduce(f32[13]{0:T(128)S(1)} %psum.60), channel_id=1, replica_groups=mesh['row'=16,'col'=16] {'row'}, use_global_device_ids=true, to_apply=%region_29.0 | all-reduce | flops 13 | bytes 104 | tf_op jit(solution)/shard_map/psum | solution.py:15
  538.2 1.5 scatter.70
  541.9 1.8 dynamic-slice.126
  545.5 1.3 scatter.76
  553.0 2.7 subtract_divide_fusion
  557.4 1.5 reshape.713
  558.8 35.8 %all_to_all.16 = bf16[16,2,16384]{2,1,0:T(2,128)(2,1)} all-to-all(bf16[16,2,16384]{2,1,0:T(2,128)(2,1)S(1)} %reshape.713), channel_id=1, replica_groups=mesh['row'=16,'col'=16] {'row'}, dimensions={0} | all-to-all | bytes 2097152 | tf_op jit(solution)/shard_map/all_to_all | solution.py:45
  594.6 4.5 reshape.714
  599.1 1.3 reshape.600
  600.4 3.8 fusion.20
  604.2 3.6 reshape.569
  607.8 3.1 fusion.15
  610.9 5.8 copy.66
  616.7 4.6 fusion.1
  621.3 3.2 copy.105
  624.5 5.6 reshape.707
  631.3 1.3 scatter.64
  632.7 1.3 scatter.85
  634.0 66.6 %reduce-scatter.14.cloned.1.call-done = f32[64,512]{1,0:T(8,128)} async-done(((f32[1024,512]{1,0:T(8,128)}), f32[64,512]{1,0:T(8,128)}) %reduce-scatter.14.cloned.1.call-update) | async-done | bytes 131088
  700.6 1.1 reshape.708
  702.7 5.7 stack.235
  708.6 30.9 %psum.62 = f32[9]{0:T(128)S(1)} all-reduce(f32[9]{0:T(128)S(1)} %stack.235), channel_id=1, replica_groups=mesh['row'=16,'col'=16] {'col'}, use_global_device_ids=true, to_apply=%region_45.0 | all-reduce | flops 9 | bytes 72 | tf_op jit(solution)/shard_map/psum | solution.py:15
  739.6 32.9 %psum.63 = f32[9]{0:T(128)S(1)} all-reduce(f32[9]{0:T(128)S(1)} %psum.62), channel_id=1, replica_groups=mesh['row'=16,'col'=16] {'row'}, use_global_device_ids=true, to_apply=%region_46.0 | all-reduce | flops 9 | bytes 72 | tf_op jit(solution)/shard_map/psum | solution.py:15
  780.5 3.9 multiply_add_fusion
  (136 shorter events, 28.7 us)
Async XLA Ops:
  7.2 116.5 %all-gather.3.cloned.1.call-start = ((), (), s32[]{:S(2)}) async-start(), calls=%async_computation.6 | async-start | bytes 2228224 | tf_op jit(solution)/shard_map/all_gather | solution.py:39
  7.9 139.5 %all-gather.5.cloned.1.call-start = ((), (), s32[]{:S(2)}) async-start(), calls=%async_computation.7 | async-start | bytes 2228224 | tf_op jit(solution)/shard_map/all_gather | solution.py:40
  83.9 8.9 %copy-start.7 = (bf16[16,16,4,4]{1,3,2,0:T(4,128)(2,1)S(1)}, bf16[16,16,4,4]{1,3,2,0:T(4,128)(2,1)}, u32[]{:S(2)}) copy-start(bf16[16,16,4,4]{1,3,2,0:T(4,128)(2,1)} %param.46) | copy-start | bytes 24580
  86.2 34.8 %all-to-all-start = ((bf16[16,2,16384]{2,1,0:T(2,128)(2,1)}), bf16[16,2,16384]{2,1,0:T(2,128)(2,1)S(1)}, u32[]{:S(2)}, u32[]{:S(2)}) async-start(bf16[16,2,16384]{2,1,0:T(2,128)(2,1)} %reshape.709), calls=%async_computation | async-start | bytes 2097152 | tf_op jit(solution)/shard_map/all_to_all | solution.py:45
  92.2 142.5 %reduce-scatter.10.cloned.1.call-start = ((), (), s32[]{:S(2)}) async-start(), calls=%async_computation.8 | async-start | bytes 2228224
  93.0 46.8 %copy-start.8 = (bf16[16,16,4,4,1,1]{0,1,2,3,5,4:T(8,128)(2,1)}, bf16[16,16,4,4,1,1]{0,1,2,3,5,4:T(8,128)(2,1)S(1)}, u32[]{:S(2)}) copy-start(bf16[16,16,4,4,1,1]{0,1,2,3,5,4:T(8,128)(2,1)S(1)} %copy.71) | copy-start | bytes 24580
  132.9 2.2 copy-start.6
  160.8 75.1 %copy-start.11 = (f32[4]{0:T(128)S(1)}, f32[4]{0:T(128)}, u32[]{:S(2)}) copy-start(f32[4]{0:T(128)} %param.47) | copy-start | bytes 52
  160.8 75.2 %copy-start = (bf16[64,4,64]{2,1,0:T(4,128)(2,1)S(1)}, bf16[64,4,64]{2,1,0:T(4,128)(2,1)}, u32[]{:S(2)}) copy-start(bf16[64,4,64]{2,1,0:T(4,128)(2,1)} %param.42) | copy-start | bytes 98308
  160.8 75.2 %copy-start.1 = (bf16[64,4,64]{2,1,0:T(4,128)(2,1)S(1)}, bf16[64,4,64]{2,1,0:T(4,128)(2,1)}, u32[]{:S(2)}) copy-start(bf16[64,4,64]{2,1,0:T(4,128)(2,1)} %param.43) | copy-start | bytes 98308
  160.8 300.8 %reduce-scatter.12.cloned.1.call-start = ((), (), s32[]{:S(2)}) async-start(), calls=%async_computation.9 | async-start | bytes 2228224
  365.2 3.6 copy-start.9
  391.1 309.4 %reduce-scatter.14.cloned.1.call-start = ((), (), s32[]{:S(2)}) async-start(), calls=%async_computation.10 | async-start | bytes 2228224
  555.8 0.7 copy-start.2
  555.8 0.7 copy-start.4
  604.2 3.6 copy-start.10
  630.1 71.7 %copy-start.3 = (f32[64,4,64]{2,0,1:T(8,128)S(1)}, f32[64,4,64]{2,0,1:T(8,128)}, u32[]{:S(2)}) copy-start(f32[64,4,64]{2,0,1:T(8,128)} %copy-done.2) | copy-start | bytes 196612
  630.1 71.7 %copy-start.5 = (f32[64,4,64]{2,0,1:T(8,128)S(1)}, f32[64,4,64]{2,0,1:T(8,128)}, u32[]{:S(2)}) copy-start(f32[64,4,64]{2,0,1:T(8,128)} %copy-done.4) | copy-start | bytes 196612
  630.1 142.6 %copy-start.12 = (f32[3,1]{0,1:T(1,128)S(1)}, f32[3,1]{0,1:T(1,128)}, u32[]{:S(2)}) copy-start(f32[3,1]{0,1:T(1,128)} %constant.468) | copy-start | bytes 40
Sparse Core Ops, SparseCore 0:
  10.5 52.1 all-gather.2
  64.5 49.4 all-gather.4
  161.0 73.7 reduce-scatter.9
  391.3 70.2 reduce-scatter.11
  630.3 70.2 reduce-scatter.13
